TPU v7x, 512 devices: a whole 4x8x8 slice. The times are simulated.
512 devices in a mesh: gx: 32 (over x, y), gy: 16 (over z, core).
Axes of the slice: x: 4, y: 8, z: 8, core: 2. Of those that a mesh axis runs over, the one named last changes fastest.
Arguments:
- right_side: bfloat16 [32, 16, 896, 128], P('gx', 'gy')
- schur_offdiag: bfloat16 [32, 16, 896, 896], P('gx', 'gy'), may hold values from -0.125 to 0.125
- schur_diag: float32 [32, 16, 896], P('gx', 'gy'), may hold values from 1.5 to 3
- trace_offdiag: bfloat16 [32, 16, 896, 896], P('gx', 'gy'), may hold values from -0.0390625 to 0.0390625
- trace_diag: float32 [32, 16, 896], P('gx', 'gy'), may hold values from 0.3 to 0.7
- couplings: bfloat16 [32, 16, 4, 128, 128], P('gx', 'gy'), may hold values from -0.375 to 0.375
- margin_rows: int32 [32, 16, 4, 128], P('gx', 'gy'), may hold values from 0 to 895, as said below
- deflation: bfloat16 [32, 16, 8, 896], P('gx', 'gy'), may hold values from -0.59765625 to 0.59765625
- coarse_inverse: float32 [4096, 4096], P(('gx', 'gy'))
- coarse_map: int32 [4096], replicated, may hold values from 0 to 4095, each once
Outputs:
- solution: float32 [32, 16, 896, 128], P('gx', 'gy')
- residual: float32 [32, 16, 896, 128], P('gx', 'gy')
Inputs may be any that keep to these rules, and one draw needn't show every extreme that they name: `margin_rows`: the 512 rows of one subdomain's four lists are all distinct. `coarse_map`: every coarse number appears once.
All inputs are finite; a program needn't handle non-finite values.
Results may differ from a plain program's by a relative error of at most 0.022.
Values may be sent and summed in bfloat16 or wider, within the bound.
No kernel may reach another device: no remote copies, remote signals or barrier semaphores. Data moves between devices by JAX's collectives and lax.ppermute only.
A program may use at most 64 MiB of HBM per device.

v0:
```python
import jax
import jax.numpy as jnp
from jax import lax
from jax.sharding import PartitionSpec as P

ITERS = 3


def from_behind(value, axis, steps):
    count = lax.axis_size(axis)
    leading, last = (max(0, -steps), min(count, count - steps))
    return lax.ppermute(value, axis, [(source, source + steps) for source in range(leading, last)])


def gather_rows(value, axis):
    count = lax.axis_size(axis)
    copies = jnp.broadcast_to(value[None], (count,) + value.shape)
    return lax.all_to_all(copies.reshape((-1,) + value.shape[1:]), axis, 0, 0, tiled=True)


def total_over_mesh(value, tie):
    for axis in ("gy", "gx"):
        if axis == "gx":
            value = value + 0.0 * tie
        count = lax.axis_size(axis)
        value = jnp.sum(gather_rows(value, axis).reshape((count,) + value.shape), axis=0)
    return value


def pass_columns(rows, offset):
    return from_behind(rows, "gx", offset)


def pass_lines(rows, offset):
    return from_behind(rows, "gy", offset)


def shards(
    right_side,
    schur_offdiag,
    schur_diag,
    trace_offdiag,
    trace_diag,
    couplings,
    margin_rows,
    deflation,
    coarse_inverse,
    coarse_map,
):
    rhs_wide = right_side[0, 0].astype(jnp.float32)
    schur_mat = schur_offdiag[0, 0]
    schur_scale = schur_diag[0, 0][:, None]
    trace_mat = trace_offdiag[0, 0]
    trace_scale = trace_diag[0, 0][:, None]
    coupling_blocks = couplings[0, 0]
    rows_lists = margin_rows[0, 0]
    sides, width = (coupling_blocks.shape[0], coupling_blocks.shape[-1])
    selectors = (
        rows_lists[:, None, :]
        == jnp.arange(schur_mat.shape[0], dtype=rows_lists.dtype)[None, :, None]
    ).astype(coupling_blocks.dtype)
    placed_couplings = (
        jnp.einsum("dra,dab->rdb", selectors, coupling_blocks, preferred_element_type=jnp.float32)
        .astype(coupling_blocks.dtype)
        .reshape(schur_mat.shape[0], sides * width)
    )
    schur_with_couplings = jnp.concatenate([schur_mat, -placed_couplings], axis=1)
    vectors = deflation[0, 0]
    vectors_wide = vectors.astype(jnp.float32).T
    trace_with_vectors = jnp.concatenate([vectors, trace_mat], axis=0)
    count_x, count_y = (lax.axis_size("gx"), lax.axis_size("gy"))
    depth = vectors.shape[0]
    coarse_cols = jnp.take(coarse_inverse, coarse_map, axis=1)
    coarse_block = lax.all_to_all(
        coarse_cols.reshape(depth, count_x, count_y * depth), "gx", 1, 0, tiled=True
    ).reshape(count_x * depth, count_y * depth)

    def exchange(sent_rows):
        return jnp.stack(
            [
                pass_columns(sent_rows[1], 1),
                pass_columns(sent_rows[0], -1),
                pass_lines(sent_rows[3], 1),
                pass_lines(sent_rows[2], -1),
            ]
        )

    def finish_schur(rounded, received):
        stacked = jnp.concatenate([rounded, received.reshape(-1, received.shape[-1])], axis=0)
        return schur_scale * rounded.astype(jnp.float32) + jnp.dot(
            schur_with_couplings, stacked, preferred_element_type=jnp.float32
        )

    def apply_schur(field):
        rounded = lax.optimization_barrier(field.astype(jnp.bfloat16))
        return finish_schur(rounded, exchange(rounded[rows_lists]))

    def send_early(base, step):
        return exchange(jnp.stack([base[rows_lists], step[rows_lists]], axis=1))

    def apply_schur_late(field, pair, coef):
        rounded = lax.optimization_barrier(field.astype(jnp.bfloat16))
        received = (pair[:, 0] + coef * pair[:, 1]).astype(jnp.bfloat16)
        return finish_schur(rounded, received)

    def apply_prec(field):
        rounded = lax.optimization_barrier(field.astype(jnp.bfloat16))
        both = jnp.dot(trace_with_vectors, rounded, preferred_element_type=jnp.float32)
        coarse = both[: vectors.shape[0]]
        result = trace_scale * rounded.astype(jnp.float32) + both[vectors.shape[0] :]
        line = gather_rows(coarse, "gy")
        partial = jnp.dot(coarse_block, line, precision=lax.Precision.HIGH)
        pieces = lax.all_to_all(partial, "gx", 0, 0, tiled=True)
        solved = jnp.sum(pieces.reshape(count_x, depth, pieces.shape[-1]), axis=0)
        return result + jnp.dot(vectors_wide, solved, precision=lax.Precision.HIGH)

    solution = jnp.zeros(rhs_wide.shape, jnp.float32)
    direction = apply_prec(rhs_wide)
    image = apply_schur(direction)
    for iteration in range(ITERS):
        mapped = apply_prec(image)
        if iteration + 1 < ITERS:
            pair = send_early(direction, mapped)
        else:
            pair = send_early(solution, direction)
        numer, denom = total_over_mesh(
            jnp.stack([jnp.sum(mapped * direction, axis=0), jnp.sum(mapped * mapped, axis=0)]),
            jnp.sum(pair[:, 0, 0, 0]),
        )
        alpha = numer / denom
        solution = solution + alpha * direction
        direction = direction + -alpha * mapped
        if iteration + 1 < ITERS:
            image = apply_schur_late(direction, pair, -alpha)
    residual = rhs_wide - apply_schur_late(solution, pair, alpha)
    return (solution[None, None], residual[None, None])


def solution(mesh):
    return jax.shard_map(
        shards,
        mesh=mesh,
        in_specs=(
            P("gx", "gy", None, None),
            P("gx", "gy", None, None),
            P("gx", "gy", None),
            P("gx", "gy", None, None),
            P("gx", "gy", None),
            P("gx", "gy", None, None, None),
            P("gx", "gy", None, None),
            P("gx", "gy", None, None),
            P(("gx", "gy"), None),
            P(),
        ),
        out_specs=(P("gx", "gy", None, None), P("gx", "gy", None, None)),
        check_vma=False,
    )
```

profile of v0, /device:TPU:1, one launch (start us, length us, event | category | flops | bytes accessed | tf_op | source)
XLA Modules:
  0.0 295.0 jit_solution(1990099982153562167)
XLA Ops:
  0.7 2.1 fusion.81
  3.4 11.8 %all-to-all-start.1 = ((f32[16,8,128]{2,1,0:T(8,128)}), f32[16,8,128]{2,1,0:T(8,128)S(1)}, u32[]{:S(2)}, u32[]{:S(2)}) async-start(f32[16,8,128]{2,1,0:T(8,128)} %broadcast_in_dim.42), calls=%async_computation.1 | async-start | bytes 131072 | tf_op jit(solution)/shard_map/all_to_all | solution.py:18
  16.0 14.1 %gather_fusion = f32[4096,8]{1,0:T(8,128)} fusion(f32[8,4096]{0,1:T(8,128)S(1)} %copy.80, s32[4096]{0:T(1024)S(1)} %fusion.67), kind=kCustom, calls=%fused_computation | custom fusion | bytes 278528 | tf_op jit(solution)/shard_map/jit(_take)/gather | solution.py:73
  30.1 2.2 copy.81
  32.9 9.7 %all-to-all-start = ((f32[8,32,128]{2,0,1:T(8,128)}), f32[8,32,128]{2,0,1:T(8,128)S(1)}, u32[]{:S(2)}, u32[]{:S(2)}) async-start(f32[8,32,128]{2,0,1:T(8,128)} %broadcast_select_fusion), calls=%async_computation | async-start | bytes 262144 | tf_op jit(solution)/shard_map/all_to_all | solution.py:74
  42.7 9.1 %all-to-all-done = f32[8,32,128]{2,0,1:T(8,128)S(1)} async-done(((f32[8,32,128]{2,0,1:T(8,128)}), f32[8,32,128]{2,0,1:T(8,128)S(1)}, u32[]{:S(2)}, u32[]{:S(2)}) %all-to-all-start) | async-done | bytes 131104 | tf_op jit(solution)/shard_map/all_to_all | solution.py:74
  52.7 4.5 %all-to-all-start.2 = ((f32[32,8,128]{2,1,0:T(8,128)}), f32[32,8,128]{2,1,0:T(8,128)S(1)}, u32[]{:S(2)}, u32[]{:S(2)}) async-start(f32[32,8,128]{2,1,0:T(8,128)} %fusion.60), calls=%async_computation.2 | async-start | bytes 262144 | tf_op jit(solution)/shard_map/all_to_all | solution.py:113
  57.2 9.1 %all-to-all-done.2 = f32[32,8,128]{2,1,0:T(8,128)S(1)} async-done(((f32[32,8,128]{2,1,0:T(8,128)}), f32[32,8,128]{2,1,0:T(8,128)S(1)}, u32[]{:S(2)}, u32[]{:S(2)}) %all-to-all-start.2) | async-done | bytes 131104 | tf_op jit(solution)/shard_map/all_to_all | solution.py:113
  66.8 1.3 gather_fusion.1
  68.1 4.6 %collective-permute-start.3 = (bf16[128,128]{1,0:T(8,128)(2,1)S(1)}, bf16[128,128]{1,0:T(8,128)(2,1)S(1)}, u32[]{:S(2)}, u32[]{:S(2)}) collective-permute-start(bf16[128,128]{1,0:T(8,128)(2,1)S(1)} %get-tuple-element.40), channel_id=1, source_target_pairs={{1,0},{2,1},{3,2},{4,3},{5,4},{6,5},{7,6},{8,7},{9,8},{10,9},{11,1... | collective-permute-start | bytes 98312 | tf_op jit(solution)/shard_map/ppermute | solution.py:12
  72.8 3.2 %collective-permute-start.2 = (bf16[128,128]{1,0:T(8,128)(2,1)S(1)}, bf16[128,128]{1,0:T(8,128)(2,1)S(1)}, u32[]{:S(2)}, u32[]{:S(2)}) collective-permute-start(bf16[128,128]{1,0:T(8,128)(2,1)S(1)} %get-tuple-element.38), channel_id=1, source_target_pairs={{0,1},{1,2},{2,3},{3,4},{4,5},{5,6},{6,7},{7,8},{8,9},{9,10},{10,1... | collective-permute-start | bytes 98312 | tf_op jit(solution)/shard_map/ppermute | solution.py:12
  76.0 1.3 collective-permute-start.1
  77.3 4.0 %collective-permute-start = (bf16[128,128]{1,0:T(8,128)(2,1)S(1)}, bf16[128,128]{1,0:T(8,128)(2,1)S(1)}, u32[]{:S(2)}, u32[]{:S(2)}) collective-permute-start(bf16[128,128]{1,0:T(8,128)(2,1)S(1)} %get-tuple-element.37), channel_id=1, source_target_pairs={{0,16},{16,32},{32,48},{48,64},{64,80},{80,96},{96,112},{112,128},... | collective-permute-start | bytes 98312 | tf_op jit(solution)/shard_map/ppermute | solution.py:12
  82.6 2.5 fusion.9
  85.8 14.4 %all_to_all.111 = f32[16,8,128]{2,1,0:T(8,128)S(1)} all-to-all(f32[16,8,128]{2,1,0:T(8,128)S(1)} %broadcast_in_dim.43), channel_id=1, replica_groups=mesh['gx'=32,'gy'=16] {'gy'}, dimensions={0} | all-to-all | bytes 131072 | tf_op jit(solution)/shard_map/all_to_all | solution.py:18
  101.1 7.3 %all-to-all-start.4 = ((f32[32,8,128]{2,1,0:T(8,128)}), f32[32,8,128]{2,1,0:T(8,128)S(1)}, u32[]{:S(2)}, u32[]{:S(2)}) async-start(f32[32,8,128]{2,1,0:T(8,128)} %fusion.58), calls=%async_computation.4 | async-start | bytes 262144 | tf_op jit(solution)/shard_map/all_to_all | solution.py:113
  109.4 8.1 %all-to-all-done.4 = f32[32,8,128]{2,1,0:T(8,128)S(1)} async-done(((f32[32,8,128]{2,1,0:T(8,128)}), f32[32,8,128]{2,1,0:T(8,128)S(1)}, u32[]{:S(2)}, u32[]{:S(2)}) %all-to-all-start.4) | async-done | bytes 131104 | tf_op jit(solution)/shard_map/all_to_all | solution.py:113
  119.1 4.0 %collective-permute-start.7 = (f32[2,128,128]{2,1,0:T(8,128)S(1)}, f32[2,128,128]{2,1,0:T(8,128)S(1)}, u32[]{:S(2)}, u32[]{:S(2)}) collective-permute-start(f32[2,128,128]{2,1,0:T(8,128)S(1)} %get-tuple-element.34), channel_id=1, source_target_pairs={{1,0},{2,1},{3,2},{4,3},{5,4},{6,5},{7,6},{8,7},{9,8},{10,9},{11,1... | collective-permute-start | bytes 393224 | tf_op jit(solution)/shard_map/ppermute | solution.py:12
  123.1 2.0 collective-permute-start.6
  125.1 1.3 collective-permute-start.5
  126.4 4.0 %collective-permute-start.4 = (f32[2,128,128]{2,1,0:T(8,128)S(1)}, f32[2,128,128]{2,1,0:T(8,128)S(1)}, u32[]{:S(2)}, u32[]{:S(2)}) collective-permute-start(f32[2,128,128]{2,1,0:T(8,128)S(1)} %get-tuple-element.32), channel_id=1, source_target_pairs={{0,16},{16,32},{32,48},{48,64},{64,80},{80,96},{96,112},{112,128},... | collective-permute-start | bytes 393224 | tf_op jit(solution)/shard_map/ppermute | solution.py:12
  130.4 10.8 %all_to_all.112 = f32[16,2,128]{2,1,0:T(2,128)S(1)} all-to-all(f32[16,2,128]{2,1,0:T(2,128)S(1)} %broadcast_in_dim.44), channel_id=1, replica_groups=mesh['gx'=32,'gy'=16] {'gy'}, dimensions={0} | all-to-all | bytes 32768 | tf_op jit(solution)/shard_map/all_to_all | solution.py:18
  143.2 4.8 %all-to-all-start.6 = ((f32[32,2,128]{2,1,0:T(2,128)}), f32[32,2,128]{2,1,0:T(2,128)S(1)}, u32[]{:S(2)}, u32[]{:S(2)}) async-start(f32[32,2,128]{2,1,0:T(2,128)} %broadcast_in_dim.45), calls=%async_computation.6 | async-start | bytes 65536 | tf_op jit(solution)/shard_map/all_to_all | solution.py:18
  148.1 8.7 %all-to-all-done.6 = f32[32,2,128]{2,1,0:T(2,128)S(1)} async-done(((f32[32,2,128]{2,1,0:T(2,128)}), f32[32,2,128]{2,1,0:T(2,128)S(1)}, u32[]{:S(2)}, u32[]{:S(2)}) %all-to-all-start.6) | async-done | bytes 32800 | tf_op jit(solution)/shard_map/all_to_all | solution.py:18
  157.0 1.3 copy-done.13
  158.3 2.1 fusion.10
  161.1 12.0 %all_to_all.113 = f32[16,8,128]{2,1,0:T(8,128)S(1)} all-to-all(f32[16,8,128]{2,1,0:T(8,128)S(1)} %broadcast_in_dim.46), channel_id=1, replica_groups=mesh['gx'=32,'gy'=16] {'gy'}, dimensions={0} | all-to-all | bytes 131072 | tf_op jit(solution)/shard_map/all_to_all | solution.py:18
  174.0 3.9 %all-to-all-start.8 = ((f32[32,8,128]{2,1,0:T(8,128)}), f32[32,8,128]{2,1,0:T(8,128)S(1)}, u32[]{:S(2)}, u32[]{:S(2)}) async-start(f32[32,8,128]{2,1,0:T(8,128)} %fusion.56), calls=%async_computation.8 | async-start | bytes 262144 | tf_op jit(solution)/shard_map/all_to_all | solution.py:113
  178.9 8.1 %all-to-all-done.8 = f32[32,8,128]{2,1,0:T(8,128)S(1)} async-done(((f32[32,8,128]{2,1,0:T(8,128)}), f32[32,8,128]{2,1,0:T(8,128)S(1)}, u32[]{:S(2)}, u32[]{:S(2)}) %all-to-all-start.8) | async-done | bytes 131104 | tf_op jit(solution)/shard_map/all_to_all | solution.py:113
  188.5 3.9 %collective-permute-start.11 = (f32[2,128,128]{2,1,0:T(8,128)S(1)}, f32[2,128,128]{2,1,0:T(8,128)S(1)}, u32[]{:S(2)}, u32[]{:S(2)}) collective-permute-start(f32[2,128,128]{2,1,0:T(8,128)S(1)} %get-tuple-element.28), channel_id=1, source_target_pairs={{1,0},{2,1},{3,2},{4,3},{5,4},{6,5},{7,6},{8,7},{9,8},{10,9},{11,1... | collective-permute-start | bytes 393224 | tf_op jit(solution)/shard_map/ppermute | solution.py:12
  192.5 2.1 collective-permute-start.10
  194.5 1.3 collective-permute-start.9
  195.8 4.0 %collective-permute-start.8 = (f32[2,128,128]{2,1,0:T(8,128)S(1)}, f32[2,128,128]{2,1,0:T(8,128)S(1)}, u32[]{:S(2)}, u32[]{:S(2)}) collective-permute-start(f32[2,128,128]{2,1,0:T(8,128)S(1)} %get-tuple-element.26), channel_id=1, source_target_pairs={{0,16},{16,32},{32,48},{48,64},{64,80},{80,96},{96,112},{112,128},... | collective-permute-start | bytes 393224 | tf_op jit(solution)/shard_map/ppermute | solution.py:12
  199.9 10.7 %all_to_all.114 = f32[16,2,128]{2,1,0:T(2,128)S(1)} all-to-all(f32[16,2,128]{2,1,0:T(2,128)S(1)} %broadcast_in_dim.47), channel_id=1, replica_groups=mesh['gx'=32,'gy'=16] {'gy'}, dimensions={0} | all-to-all | bytes 32768 | tf_op jit(solution)/shard_map/all_to_all | solution.py:18
  212.6 5.2 %all-to-all-start.10 = ((f32[32,2,128]{2,1,0:T(2,128)}), f32[32,2,128]{2,1,0:T(2,128)S(1)}, u32[]{:S(2)}, u32[]{:S(2)}) async-start(f32[32,2,128]{2,1,0:T(2,128)} %broadcast_in_dim.48), calls=%async_computation.10 | async-start | bytes 65536 | tf_op jit(solution)/shard_map/all_to_all | solution.py:18
  217.8 8.7 %all-to-all-done.10 = f32[32,2,128]{2,1,0:T(2,128)S(1)} async-done(((f32[32,2,128]{2,1,0:T(2,128)}), f32[32,2,128]{2,1,0:T(2,128)S(1)}, u32[]{:S(2)}, u32[]{:S(2)}) %all-to-all-start.10) | async-done | bytes 32800 | tf_op jit(solution)/shard_map/all_to_all | solution.py:18
  228.0 2.1 fusion.11
  230.8 12.0 %all_to_all.115 = f32[16,8,128]{2,1,0:T(8,128)S(1)} all-to-all(f32[16,8,128]{2,1,0:T(8,128)S(1)} %broadcast_in_dim.49), channel_id=1, replica_groups=mesh['gx'=32,'gy'=16] {'gy'}, dimensions={0} | all-to-all | bytes 131072 | tf_op jit(solution)/shard_map/all_to_all | solution.py:18
  243.7 3.9 %all-to-all-start.12 = ((f32[32,8,128]{2,1,0:T(8,128)}), f32[32,8,128]{2,1,0:T(8,128)S(1)}, u32[]{:S(2)}, u32[]{:S(2)}) async-start(f32[32,8,128]{2,1,0:T(8,128)} %fusion.54), calls=%async_computation.12 | async-start | bytes 262144 | tf_op jit(solution)/shard_map/all_to_all | solution.py:113
  250.3 2.0 collective-permute-start.15
  252.4 3.5 %collective-permute-start.14 = (f32[2,128,128]{2,1,0:T(8,128)S(1)}, f32[2,128,128]{2,1,0:T(8,128)S(1)}, u32[]{:S(2)}, u32[]{:S(2)}) collective-permute-start(f32[2,128,128]{2,1,0:T(8,128)S(1)} %get-tuple-element.23), channel_id=1, source_target_pairs={{0,1},{1,2},{2,3},{3,4},{4,5},{5,6},{6,7},{7,8},{8,9},{9,10},{10,1... | collective-permute-start | bytes 393224 | tf_op jit(solution)/shard_map/ppermute | solution.py:12
  255.9 1.3 collective-permute-start.13
  257.2 4.0 %collective-permute-start.12 = (f32[2,128,128]{2,1,0:T(8,128)S(1)}, f32[2,128,128]{2,1,0:T(8,128)S(1)}, u32[]{:S(2)}, u32[]{:S(2)}) collective-permute-start(f32[2,128,128]{2,1,0:T(8,128)S(1)} %get-tuple-element.20), channel_id=1, source_target_pairs={{0,16},{16,32},{32,48},{48,64},{64,80},{80,96},{96,112},{112,128},... | collective-permute-start | bytes 393224 | tf_op jit(solution)/shard_map/ppermute | solution.py:12
  262.3 3.5 %all-to-all-start.13 = ((f32[16,2,128]{2,1,0:T(2,128)}), f32[16,2,128]{2,1,0:T(2,128)S(1)}, u32[]{:S(2)}, u32[]{:S(2)}) async-start(f32[16,2,128]{2,1,0:T(2,128)} %broadcast_in_dim.50), calls=%async_computation.13 | async-start | bytes 32768 | tf_op jit(solution)/shard_map/all_to_all | solution.py:18
  267.2 6.0 %all-to-all-done.13 = f32[16,2,128]{2,1,0:T(2,128)S(1)} async-done(((f32[16,2,128]{2,1,0:T(2,128)}), f32[16,2,128]{2,1,0:T(2,128)S(1)}, u32[]{:S(2)}, u32[]{:S(2)}) %all-to-all-start.13) | async-done | bytes 16416 | tf_op jit(solution)/shard_map/all_to_all | solution.py:18
  273.8 9.2 %all-to-all-start.14 = ((f32[32,2,128]{2,1,0:T(2,128)}), f32[32,2,128]{2,1,0:T(2,128)S(1)}, u32[]{:S(2)}, u32[]{:S(2)}) async-start(f32[32,2,128]{2,1,0:T(2,128)} %broadcast_in_dim.51), calls=%async_computation.14 | async-start | bytes 65536 | tf_op jit(solution)/shard_map/all_to_all | solution.py:18
  283.1 8.7 %all-to-all-done.14 = f32[32,2,128]{2,1,0:T(2,128)S(1)} async-done(((f32[32,2,128]{2,1,0:T(2,128)}), f32[32,2,128]{2,1,0:T(2,128)S(1)}, u32[]{:S(2)}, u32[]{:S(2)}) %all-to-all-start.14) | async-done | bytes 32800 | tf_op jit(solution)/shard_map/all_to_all | solution.py:18
  293.4 1.6 fusion.4
  (129 shorter events, 25.3 us)
Async XLA Ops:
  0.6 80.7 %copy-start = (bf16[1,1,4,128,128]{4,3,2,1,0:T(8,128)(2,1)S(1)}, bf16[1,1,4,128,128]{4,3,2,1,0:T(8,128)(2,1)}, u32[]{:S(2)}) copy-start(bf16[1,1,4,128,128]{4,3,2,1,0:T(8,128)(2,1)} %param.15) | copy-start | bytes 393220
  0.6 14.6 %copy-start.6 = (s32[4096]{0:T(1024)S(1)}, s32[4096]{0:T(1024)}, u32[]{:S(2)}) copy-start(s32[4096]{0:T(1024)} %param.19) | copy-start | bytes 49156
  0.7 14.7 %copy-start.5 = (f32[8,4096]{1,0:T(8,128)S(1)}, f32[8,4096]{1,0:T(8,128)}, u32[]{:S(2)}) copy-start(f32[8,4096]{1,0:T(8,128)} %param.18) | copy-start | bytes 393220
  3.4 29.5 %all-to-all-start.1 = ((f32[16,8,128]{2,1,0:T(8,128)}), f32[16,8,128]{2,1,0:T(8,128)S(1)}, u32[]{:S(2)}, u32[]{:S(2)}) async-start(f32[16,8,128]{2,1,0:T(8,128)} %broadcast_in_dim.42), calls=%async_computation.1 | async-start | bytes 131072 | tf_op jit(solution)/shard_map/all_to_all | solution.py:18
  15.9 26.7 %copy-start.7 = (f32[1,1,896]{2,1,0:T(1,128)S(1)}, f32[1,1,896]{2,1,0:T(1,128)}, u32[]{:S(2)}) copy-start(f32[1,1,896]{2,1,0:T(1,128)} %param.14) | copy-start | bytes 10756
  15.9 41.2 %copy-start.9 = (s32[1,1,4,128]{3,2,1,0:T(4,128)S(1)}, s32[1,1,4,128]{3,2,1,0:T(4,128)}, u32[]{:S(2)}) copy-start(s32[1,1,4,128]{3,2,1,0:T(4,128)} %param.16) | copy-start | bytes 6148
  16.0 50.4 %copy-start.3 = (bf16[1,1,8,896]{3,2,1,0:T(8,128)(2,1)S(1)}, bf16[1,1,8,896]{3,2,1,0:T(8,128)(2,1)}, u32[]{:S(2)}) copy-start(bf16[1,1,8,896]{3,2,1,0:T(8,128)(2,1)} %param.17) | copy-start | bytes 43012
  16.0 50.4 %copy-start.4 = (bf16[1,1,896,128]{3,2,1,0:T(8,128)(2,1)S(1)}, bf16[1,1,896,128]{3,2,1,0:T(8,128)(2,1)}, u32[]{:S(2)}) copy-start(bf16[1,1,896,128]{3,2,1,0:T(8,128)(2,1)} %param.10) | copy-start | bytes 688132
  32.9 18.9 %all-to-all-start = ((f32[8,32,128]{2,0,1:T(8,128)}), f32[8,32,128]{2,0,1:T(8,128)S(1)}, u32[]{:S(2)}, u32[]{:S(2)}) async-start(f32[8,32,128]{2,0,1:T(8,128)} %broadcast_select_fusion), calls=%async_computation | async-start | bytes 262144 | tf_op jit(solution)/shard_map/all_to_all | solution.py:74
  52.7 13.7 %all-to-all-start.2 = ((f32[32,8,128]{2,1,0:T(8,128)}), f32[32,8,128]{2,1,0:T(8,128)S(1)}, u32[]{:S(2)}, u32[]{:S(2)}) async-start(f32[32,8,128]{2,1,0:T(8,128)} %fusion.60), calls=%async_computation.2 | async-start | bytes 262144 | tf_op jit(solution)/shard_map/all_to_all | solution.py:113
  66.4 15.5 %copy-start.8 = (f32[1,1,896]{2,1,0:T(1,128)S(1)}, f32[1,1,896]{2,1,0:T(1,128)}, u32[]{:S(2)}) copy-start(f32[1,1,896]{2,1,0:T(1,128)} %param.12) | copy-start | bytes 10756
  68.1 14.3 %collective-permute-start.3 = (bf16[128,128]{1,0:T(8,128)(2,1)S(1)}, bf16[128,128]{1,0:T(8,128)(2,1)S(1)}, u32[]{:S(2)}, u32[]{:S(2)}) collective-permute-start(bf16[128,128]{1,0:T(8,128)(2,1)S(1)} %get-tuple-element.40), channel_id=1, source_target_pairs={{1,0},{2,1},{3,2},{4,3},{5,4},{6,5},{7,6},{8,7},{9,8},{10,9},{11,1... | collective-permute-start | bytes 98312 | tf_op jit(solution)/shard_map/ppermute | solution.py:12
  72.8 9.7 %collective-permute-start.2 = (bf16[128,128]{1,0:T(8,128)(2,1)S(1)}, bf16[128,128]{1,0:T(8,128)(2,1)S(1)}, u32[]{:S(2)}, u32[]{:S(2)}) collective-permute-start(bf16[128,128]{1,0:T(8,128)(2,1)S(1)} %get-tuple-element.38), channel_id=1, source_target_pairs={{0,1},{1,2},{2,3},{3,4},{4,5},{5,6},{6,7},{7,8},{8,9},{9,10},{10,1... | collective-permute-start | bytes 98312 | tf_op jit(solution)/shard_map/ppermute | solution.py:12
  76.0 6.5 %collective-permute-start.1 = (bf16[128,128]{1,0:T(8,128)(2,1)S(1)}, bf16[128,128]{1,0:T(8,128)(2,1)S(1)}, u32[]{:S(2)}, u32[]{:S(2)}) collective-permute-start(bf16[128,128]{1,0:T(8,128)(2,1)S(1)} %get-tuple-element.39), channel_id=1, source_target_pairs={{16,0},{32,16},{48,32},{64,48},{80,64},{96,80},{112,96},{128,112},... | collective-permute-start | bytes 98312 | tf_op jit(solution)/shard_map/ppermute | solution.py:12
  77.3 5.2 %collective-permute-start = (bf16[128,128]{1,0:T(8,128)(2,1)S(1)}, bf16[128,128]{1,0:T(8,128)(2,1)S(1)}, u32[]{:S(2)}, u32[]{:S(2)}) collective-permute-start(bf16[128,128]{1,0:T(8,128)(2,1)S(1)} %get-tuple-element.37), channel_id=1, source_target_pairs={{0,16},{16,32},{32,48},{48,64},{64,80},{80,96},{96,112},{112,128},... | collective-permute-start | bytes 98312 | tf_op jit(solution)/shard_map/ppermute | solution.py:12
  82.5 2.6 copy-start.1
  82.5 2.6 copy-start.10
  101.1 16.4 %all-to-all-start.4 = ((f32[32,8,128]{2,1,0:T(8,128)}), f32[32,8,128]{2,1,0:T(8,128)S(1)}, u32[]{:S(2)}, u32[]{:S(2)}) async-start(f32[32,8,128]{2,1,0:T(8,128)} %fusion.58), calls=%async_computation.4 | async-start | bytes 262144 | tf_op jit(solution)/shard_map/all_to_all | solution.py:113
  119.1 22.2 %collective-permute-start.7 = (f32[2,128,128]{2,1,0:T(8,128)S(1)}, f32[2,128,128]{2,1,0:T(8,128)S(1)}, u32[]{:S(2)}, u32[]{:S(2)}) collective-permute-start(f32[2,128,128]{2,1,0:T(8,128)S(1)} %get-tuple-element.34), channel_id=1, source_target_pairs={{1,0},{2,1},{3,2},{4,3},{5,4},{6,5},{7,6},{8,7},{9,8},{10,9},{11,1... | collective-permute-start | bytes 393224 | tf_op jit(solution)/shard_map/ppermute | solution.py:12
  123.1 18.2 %collective-permute-start.6 = (f32[2,128,128]{2,1,0:T(8,128)S(1)}, f32[2,128,128]{2,1,0:T(8,128)S(1)}, u32[]{:S(2)}, u32[]{:S(2)}) collective-permute-start(f32[2,128,128]{2,1,0:T(8,128)S(1)} %get-tuple-element.35), channel_id=1, source_target_pairs={{0,1},{1,2},{2,3},{3,4},{4,5},{5,6},{6,7},{7,8},{8,9},{9,10},{10,1... | collective-permute-start | bytes 393224 | tf_op jit(solution)/shard_map/ppermute | solution.py:12
  125.1 16.1 %collective-permute-start.5 = (f32[2,128,128]{2,1,0:T(8,128)S(1)}, f32[2,128,128]{2,1,0:T(8,128)S(1)}, u32[]{:S(2)}, u32[]{:S(2)}) collective-permute-start(f32[2,128,128]{2,1,0:T(8,128)S(1)} %get-tuple-element.33), channel_id=1, source_target_pairs={{16,0},{32,16},{48,32},{64,48},{80,64},{96,80},{112,96},{128,112},... | collective-permute-start | bytes 393224 | tf_op jit(solution)/shard_map/ppermute | solution.py:12
  126.4 14.8 %collective-permute-start.4 = (f32[2,128,128]{2,1,0:T(8,128)S(1)}, f32[2,128,128]{2,1,0:T(8,128)S(1)}, u32[]{:S(2)}, u32[]{:S(2)}) collective-permute-start(f32[2,128,128]{2,1,0:T(8,128)S(1)} %get-tuple-element.32), channel_id=1, source_target_pairs={{0,16},{16,32},{32,48},{48,64},{64,80},{80,96},{96,112},{112,128},... | collective-permute-start | bytes 393224 | tf_op jit(solution)/shard_map/ppermute | solution.py:12
  143.2 13.6 %all-to-all-start.6 = ((f32[32,2,128]{2,1,0:T(2,128)}), f32[32,2,128]{2,1,0:T(2,128)S(1)}, u32[]{:S(2)}, u32[]{:S(2)}) async-start(f32[32,2,128]{2,1,0:T(2,128)} %broadcast_in_dim.45), calls=%async_computation.6 | async-start | bytes 65536 | tf_op jit(solution)/shard_map/all_to_all | solution.py:18
  156.8 1.4 copy-start.13
  158.3 2.1 copy-start.11
  174.0 13.0 %all-to-all-start.8 = ((f32[32,8,128]{2,1,0:T(8,128)}), f32[32,8,128]{2,1,0:T(8,128)S(1)}, u32[]{:S(2)}, u32[]{:S(2)}) async-start(f32[32,8,128]{2,1,0:T(8,128)} %fusion.56), calls=%async_computation.8 | async-start | bytes 262144 | tf_op jit(solution)/shard_map/all_to_all | solution.py:113
  188.5 22.1 %collective-permute-start.11 = (f32[2,128,128]{2,1,0:T(8,128)S(1)}, f32[2,128,128]{2,1,0:T(8,128)S(1)}, u32[]{:S(2)}, u32[]{:S(2)}) collective-permute-start(f32[2,128,128]{2,1,0:T(8,128)S(1)} %get-tuple-element.28), channel_id=1, source_target_pairs={{1,0},{2,1},{3,2},{4,3},{5,4},{6,5},{7,6},{8,7},{9,8},{10,9},{11,1... | collective-permute-start | bytes 393224 | tf_op jit(solution)/shard_map/ppermute | solution.py:12
  192.5 18.2 %collective-permute-start.10 = (f32[2,128,128]{2,1,0:T(8,128)S(1)}, f32[2,128,128]{2,1,0:T(8,128)S(1)}, u32[]{:S(2)}, u32[]{:S(2)}) collective-permute-start(f32[2,128,128]{2,1,0:T(8,128)S(1)} %get-tuple-element.29), channel_id=1, source_target_pairs={{0,1},{1,2},{2,3},{3,4},{4,5},{5,6},{6,7},{7,8},{8,9},{9,10},{10,1... | collective-permute-start | bytes 393224 | tf_op jit(solution)/shard_map/ppermute | solution.py:12
  194.5 16.1 %collective-permute-start.9 = (f32[2,128,128]{2,1,0:T(8,128)S(1)}, f32[2,128,128]{2,1,0:T(8,128)S(1)}, u32[]{:S(2)}, u32[]{:S(2)}) collective-permute-start(f32[2,128,128]{2,1,0:T(8,128)S(1)} %get-tuple-element.27), channel_id=1, source_target_pairs={{16,0},{32,16},{48,32},{64,48},{80,64},{96,80},{112,96},{128,112},... | collective-permute-start | bytes 393224 | tf_op jit(solution)/shard_map/ppermute | solution.py:12
  195.8 14.8 %collective-permute-start.8 = (f32[2,128,128]{2,1,0:T(8,128)S(1)}, f32[2,128,128]{2,1,0:T(8,128)S(1)}, u32[]{:S(2)}, u32[]{:S(2)}) collective-permute-start(f32[2,128,128]{2,1,0:T(8,128)S(1)} %get-tuple-element.26), channel_id=1, source_target_pairs={{0,16},{16,32},{32,48},{48,64},{64,80},{80,96},{96,112},{112,128},... | collective-permute-start | bytes 393224 | tf_op jit(solution)/shard_map/ppermute | solution.py:12
  212.6 13.9 %all-to-all-start.10 = ((f32[32,2,128]{2,1,0:T(2,128)}), f32[32,2,128]{2,1,0:T(2,128)S(1)}, u32[]{:S(2)}, u32[]{:S(2)}) async-start(f32[32,2,128]{2,1,0:T(2,128)} %broadcast_in_dim.48), calls=%async_computation.10 | async-start | bytes 65536 | tf_op jit(solution)/shard_map/all_to_all | solution.py:18
  226.5 1.4 copy-start.14
  228.0 2.1 copy-start.12
  243.7 17.5 %all-to-all-start.12 = ((f32[32,8,128]{2,1,0:T(8,128)}), f32[32,8,128]{2,1,0:T(8,128)S(1)}, u32[]{:S(2)}, u32[]{:S(2)}) async-start(f32[32,8,128]{2,1,0:T(8,128)} %fusion.54), calls=%async_computation.12 | async-start | bytes 262144 | tf_op jit(solution)/shard_map/all_to_all | solution.py:113
  250.3 15.5 %collective-permute-start.15 = (f32[2,128,128]{2,1,0:T(8,128)}, f32[2,128,128]{2,1,0:T(8,128)S(1)}, u32[]{:S(2)}, u32[]{:S(2)}) collective-permute-start(f32[2,128,128]{2,1,0:T(8,128)} %get-tuple-element.22), channel_id=1, source_target_pairs={{1,0},{2,1},{3,2},{4,3},{5,4},{6,5},{7,6},{8,7},{9,8},{10,9},{11,1... | collective-permute-start | bytes 393224 | tf_op jit(solution)/shard_map/ppermute | solution.py:12
  252.4 13.4 %collective-permute-start.14 = (f32[2,128,128]{2,1,0:T(8,128)S(1)}, f32[2,128,128]{2,1,0:T(8,128)S(1)}, u32[]{:S(2)}, u32[]{:S(2)}) collective-permute-start(f32[2,128,128]{2,1,0:T(8,128)S(1)} %get-tuple-element.23), channel_id=1, source_target_pairs={{0,1},{1,2},{2,3},{3,4},{4,5},{5,6},{6,7},{7,8},{8,9},{9,10},{10,1... | collective-permute-start | bytes 393224 | tf_op jit(solution)/shard_map/ppermute | solution.py:12
  255.9 9.9 %collective-permute-start.13 = (f32[2,128,128]{2,1,0:T(8,128)S(1)}, f32[2,128,128]{2,1,0:T(8,128)S(1)}, u32[]{:S(2)}, u32[]{:S(2)}) collective-permute-start(f32[2,128,128]{2,1,0:T(8,128)S(1)} %get-tuple-element.21), channel_id=1, source_target_pairs={{16,0},{32,16},{48,32},{64,48},{80,64},{96,80},{112,96},{128,112},... | collective-permute-start | bytes 393224 | tf_op jit(solution)/shard_map/ppermute | solution.py:12
  257.2 8.6 %collective-permute-start.12 = (f32[2,128,128]{2,1,0:T(8,128)S(1)}, f32[2,128,128]{2,1,0:T(8,128)S(1)}, u32[]{:S(2)}, u32[]{:S(2)}) collective-permute-start(f32[2,128,128]{2,1,0:T(8,128)S(1)} %get-tuple-element.20), channel_id=1, source_target_pairs={{0,16},{16,32},{32,48},{48,64},{64,80},{80,96},{96,112},{112,128},... | collective-permute-start | bytes 393224 | tf_op jit(solution)/shard_map/ppermute | solution.py:12
  262.3 10.9 %all-to-all-start.13 = ((f32[16,2,128]{2,1,0:T(2,128)}), f32[16,2,128]{2,1,0:T(2,128)S(1)}, u32[]{:S(2)}, u32[]{:S(2)}) async-start(f32[16,2,128]{2,1,0:T(2,128)} %broadcast_in_dim.50), calls=%async_computation.13 | async-start | bytes 32768 | tf_op jit(solution)/shard_map/all_to_all | solution.py:18
  265.9 26.8 %copy-start.2 = (bf16[896,512]{1,0:T(8,128)(2,1)S(1)}, bf16[896,512]{1,0:T(8,128)(2,1)}, u32[]{:S(2)}) copy-start(bf16[896,512]{1,0:T(8,128)(2,1)} %copy-done.1) | copy-start | bytes 2752516
  273.8 18.0 %all-to-all-start.14 = ((f32[32,2,128]{2,1,0:T(2,128)}), f32[32,2,128]{2,1,0:T(2,128)S(1)}, u32[]{:S(2)}, u32[]{:S(2)}) async-start(f32[32,2,128]{2,1,0:T(2,128)} %broadcast_in_dim.51), calls=%async_computation.14 | async-start | bytes 65536 | tf_op jit(solution)/shard_map/all_to_all | solution.py:18
  291.8 1.6 copy-start.15
where the time goes:
time: 297 us; the launch traced here: 295 us
  starting transfers between devices  110 us (37%)
  waiting for transfers between devices  66.6 us (22%)
  blocking collectives  59.9 us (20%)
  local copies, waits for them, and re-layouts  31.5 us (11%)
  matrix products  18.1 us (6%)
  other arithmetic  4.99 us (2%)
  between operations  3.48 us (1%)
    all_to_all x5, blocking collectives, gather_rows(): lax.all_to_all(copies.reshape((-1,) + value.shape[1:]), axis, 0, 0, tiled...  59.9 us
    ppermute x16, starting transfers between devices, from_behind(): lax.ppermute(value, axis, [(source, source + steps) for source in range(l...  46.6 us
    all_to_all x5, starting transfers between devices, gather_rows(): lax.all_to_all(copies.reshape((-1,) + value.shape[1:]), axis, 0, 0, tiled...  34.5 us
    all_to_all x5, waiting for transfers between devices, gather_rows(): lax.all_to_all(copies.reshape((-1,) + value.shape[1:]), axis, 0, 0, tiled...  32.1 us
    all_to_all x4, waiting for transfers between devices, apply_prec(): pieces = lax.all_to_all(partial, 'gx', 0, 0, tiled=True)  25.3 us
    all_to_all x4, starting transfers between devices, apply_prec(): pieces = lax.all_to_all(partial, 'gx', 0, 0, tiled=True)  19.5 us
    gather x2, local copies, waits for them, and re-layouts, shards(): coarse_cols = jnp.take(coarse_inverse, coarse_map, axis=1)  16.3 us
    all_to_all x1, starting transfers between devices, shards(): lax.all_to_all(coarse_cols.reshape(depth, count_x, count_y * depth), 'gx'...  9.69 us
  transfers between devices with their start and end apart: 26, of which 8 were waited for; matrix products, arithmetic and copies ran while one was open for 9% of the time, Pallas kernels for 0%

commit v1 on v0

--- a/solution.py
+++ b/solution.py
@@ -71,8 +71,20 @@
     count_x, count_y = (lax.axis_size("gx"), lax.axis_size("gy"))
     depth = vectors.shape[0]
     coarse_cols = jnp.take(coarse_inverse, coarse_map, axis=1)
-    coarse_block = lax.all_to_all(
-        coarse_cols.reshape(depth, count_x, count_y * depth), "gx", 1, 0, tiled=True
+    coarse_block = jnp.concatenate(
+        lax.all_to_all(
+            jnp.stack(
+                jnp.split(
+                    coarse_cols.reshape(depth, count_x, count_y * depth),
+                    lax.axis_size("gx"),
+                    axis=1,
+                )
+            ),
+            "gx",
+            0,
+            0,
+        ),
+        axis=0,
     ).reshape(count_x * depth, count_y * depth)
 
     def exchange(sent_rows):

time: 297 us -> 315 us (1.061)
  local copies, waits for them, and re-layouts: 31.5 us -> 50.6 us
    unnamed x33 -> x64, local copies, waits for them, and re-layouts: 3.89 us -> 22.3 us
  transfers between devices with their start and end apart: 26 -> 26, of which waited for: 8 -> 8; matrix products, arithmetic and copies ran while one was open for 9% -> 14% of each run, Pallas kernels for 0% -> 0%
where the time goes in v1:
time: 315 us; the launch traced here: 314 us
  starting transfers between devices  111 us (35%)
  waiting for transfers between devices  66.6 us (21%)
  blocking collectives  59.9 us (19%)
  local copies, waits for them, and re-layouts  50.6 us (16%)
  matrix products  18.1 us (6%)
  other arithmetic  4.33 us (1%)
  between operations  3.48 us (1%)
    all_to_all x5, blocking collectives, gather_rows(): lax.all_to_all(copies.reshape((-1,) + value.shape[1:]), axis, 0, 0, tiled...  59.9 us
    ppermute x16, starting transfers between devices, from_behind(): lax.ppermute(value, axis, [(source, source + steps) for source in range(l...  46.7 us
    all_to_all x5, starting transfers between devices, gather_rows(): lax.all_to_all(copies.reshape((-1,) + value.shape[1:]), axis, 0, 0, tiled...  34.6 us
    all_to_all x5, waiting for transfers between devices, gather_rows(): lax.all_to_all(copies.reshape((-1,) + value.shape[1:]), axis, 0, 0, tiled...  32.1 us
    all_to_all x4, waiting for transfers between devices, apply_prec(): pieces = lax.all_to_all(partial, 'gx', 0, 0, tiled=True)  25.3 us
    unnamed x64, local copies, waits for them, and re-layouts  22.3 us
    all_to_all x4, starting transfers between devices, apply_prec(): pieces = lax.all_to_all(partial, 'gx', 0, 0, tiled=True)  19.5 us
    gather x2, local copies, waits for them, and re-layouts, shards(): coarse_cols = jnp.take(coarse_inverse, coarse_map, axis=1)  16.3 us
  transfers between devices with their start and end apart: 26, of which 8 were waited for; matrix products, arithmetic and copies ran while one was open for 14% of the time, Pallas kernels for 0%

profile of v1, /device:TPU:1, one launch (start us, length us, event | category | flops | bytes accessed | tf_op | source)
XLA Modules:
  0.0 313.6 jit_solution(10217868023461570194)
XLA Ops:
  0.7 2.1 fusion.81
  3.4 11.8 %all-to-all-start.1 = ((f32[16,8,128]{2,1,0:T(8,128)}), f32[16,8,128]{2,1,0:T(8,128)S(1)}, u32[]{:S(2)}, u32[]{:S(2)}) async-start(f32[16,8,128]{2,1,0:T(8,128)} %broadcast_in_dim.42), calls=%async_computation.1 | async-start | bytes 131072 | tf_op jit(solution)/shard_map/all_to_all | solution.py:18
  15.9 14.1 %gather_fusion = f32[4096,8]{1,0:T(8,128)} fusion(f32[8,4096]{0,1:T(8,128)S(1)} %copy.80, s32[4096]{0:T(1024)S(1)} %fusion.67), kind=kCustom, calls=%fused_computation | custom fusion | bytes 278528 | tf_op jit(solution)/shard_map/jit(_take)/gather | solution.py:73
  30.1 2.2 copy.81
  51.3 9.7 %all-to-all-start = ((f32[32,8,1,128]{3,1,2,0:T(8,128)}), f32[32,8,1,128]{3,1,2,0:T(8,128)S(1)}, u32[]{:S(2)}, u32[]{:S(2)}) async-start(f32[32,8,1,128]{3,1,2,0:T(8,128)} %constant_dynamic-update-slice_fusion), calls=%async_computation | async-start | bytes 262144 | tf_op jit(solution)/shard_map/all_to_all | solution.py:75
  61.0 9.1 %all-to-all-done = f32[32,8,1,128]{3,1,2,0:T(8,128)S(1)} async-done(((f32[32,8,1,128]{3,1,2,0:T(8,128)}), f32[32,8,1,128]{3,1,2,0:T(8,128)S(1)}, u32[]{:S(2)}, u32[]{:S(2)}) %all-to-all-start) | async-done | bytes 131104 | tf_op jit(solution)/shard_map/all_to_all | solution.py:75
  71.0 4.5 %all-to-all-start.2 = ((f32[32,8,128]{2,1,0:T(8,128)}), f32[32,8,128]{2,1,0:T(8,128)S(1)}, u32[]{:S(2)}, u32[]{:S(2)}) async-start(f32[32,8,128]{2,1,0:T(8,128)} %fusion.61), calls=%async_computation.2 | async-start | bytes 262144 | tf_op jit(solution)/shard_map/all_to_all | solution.py:125
  75.6 9.1 %all-to-all-done.2 = f32[32,8,128]{2,1,0:T(8,128)S(1)} async-done(((f32[32,8,128]{2,1,0:T(8,128)}), f32[32,8,128]{2,1,0:T(8,128)S(1)}, u32[]{:S(2)}, u32[]{:S(2)}) %all-to-all-start.2) | async-done | bytes 131104 | tf_op jit(solution)/shard_map/all_to_all | solution.py:125
  85.1 1.3 gather_fusion.1
  86.5 4.6 %collective-permute-start.3 = (bf16[128,128]{1,0:T(8,128)(2,1)S(1)}, bf16[128,128]{1,0:T(8,128)(2,1)S(1)}, u32[]{:S(2)}, u32[]{:S(2)}) collective-permute-start(bf16[128,128]{1,0:T(8,128)(2,1)S(1)} %get-tuple-element.40), channel_id=1, source_target_pairs={{1,0},{2,1},{3,2},{4,3},{5,4},{6,5},{7,6},{8,7},{9,8},{10,9},{11,1... | collective-permute-start | bytes 98312 | tf_op jit(solution)/shard_map/ppermute | solution.py:12
  91.1 3.2 %collective-permute-start.2 = (bf16[128,128]{1,0:T(8,128)(2,1)S(1)}, bf16[128,128]{1,0:T(8,128)(2,1)S(1)}, u32[]{:S(2)}, u32[]{:S(2)}) collective-permute-start(bf16[128,128]{1,0:T(8,128)(2,1)S(1)} %get-tuple-element.38), channel_id=1, source_target_pairs={{0,1},{1,2},{2,3},{3,4},{4,5},{5,6},{6,7},{7,8},{8,9},{9,10},{10,1... | collective-permute-start | bytes 98312 | tf_op jit(solution)/shard_map/ppermute | solution.py:12
  94.3 1.3 collective-permute-start.1
  95.6 4.0 %collective-permute-start = (bf16[128,128]{1,0:T(8,128)(2,1)S(1)}, bf16[128,128]{1,0:T(8,128)(2,1)S(1)}, u32[]{:S(2)}, u32[]{:S(2)}) collective-permute-start(bf16[128,128]{1,0:T(8,128)(2,1)S(1)} %get-tuple-element.37), channel_id=1, source_target_pairs={{0,16},{16,32},{32,48},{48,64},{64,80},{80,96},{96,112},{112,128},... | collective-permute-start | bytes 98312 | tf_op jit(solution)/shard_map/ppermute | solution.py:12
  100.9 2.5 fusion.9
  104.2 14.4 %all_to_all.101 = f32[16,8,128]{2,1,0:T(8,128)S(1)} all-to-all(f32[16,8,128]{2,1,0:T(8,128)S(1)} %broadcast_in_dim.43), channel_id=1, replica_groups=mesh['gx'=32,'gy'=16] {'gy'}, dimensions={0} | all-to-all | bytes 131072 | tf_op jit(solution)/shard_map/all_to_all | solution.py:18
  119.4 7.3 %all-to-all-start.4 = ((f32[32,8,128]{2,1,0:T(8,128)}), f32[32,8,128]{2,1,0:T(8,128)S(1)}, u32[]{:S(2)}, u32[]{:S(2)}) async-start(f32[32,8,128]{2,1,0:T(8,128)} %fusion.59), calls=%async_computation.4 | async-start | bytes 262144 | tf_op jit(solution)/shard_map/all_to_all | solution.py:125
  127.8 8.1 %all-to-all-done.4 = f32[32,8,128]{2,1,0:T(8,128)S(1)} async-done(((f32[32,8,128]{2,1,0:T(8,128)}), f32[32,8,128]{2,1,0:T(8,128)S(1)}, u32[]{:S(2)}, u32[]{:S(2)}) %all-to-all-start.4) | async-done | bytes 131104 | tf_op jit(solution)/shard_map/all_to_all | solution.py:125
  137.4 4.0 %collective-permute-start.7 = (f32[2,128,128]{2,1,0:T(8,128)S(1)}, f32[2,128,128]{2,1,0:T(8,128)S(1)}, u32[]{:S(2)}, u32[]{:S(2)}) collective-permute-start(f32[2,128,128]{2,1,0:T(8,128)S(1)} %get-tuple-element.34), channel_id=1, source_target_pairs={{1,0},{2,1},{3,2},{4,3},{5,4},{6,5},{7,6},{8,7},{9,8},{10,9},{11,1... | collective-permute-start | bytes 393224 | tf_op jit(solution)/shard_map/ppermute | solution.py:12
  141.5 2.0 collective-permute-start.6
  143.5 1.3 collective-permute-start.5
  144.8 4.0 %collective-permute-start.4 = (f32[2,128,128]{2,1,0:T(8,128)S(1)}, f32[2,128,128]{2,1,0:T(8,128)S(1)}, u32[]{:S(2)}, u32[]{:S(2)}) collective-permute-start(f32[2,128,128]{2,1,0:T(8,128)S(1)} %get-tuple-element.32), channel_id=1, source_target_pairs={{0,16},{16,32},{32,48},{48,64},{64,80},{80,96},{96,112},{112,128},... | collective-permute-start | bytes 393224 | tf_op jit(solution)/shard_map/ppermute | solution.py:12
  148.8 10.8 %all_to_all.102 = f32[16,2,128]{2,1,0:T(2,128)S(1)} all-to-all(f32[16,2,128]{2,1,0:T(2,128)S(1)} %broadcast_in_dim.44), channel_id=1, replica_groups=mesh['gx'=32,'gy'=16] {'gy'}, dimensions={0} | all-to-all | bytes 32768 | tf_op jit(solution)/shard_map/all_to_all | solution.py:18
  161.6 4.8 %all-to-all-start.6 = ((f32[32,2,128]{2,1,0:T(2,128)}), f32[32,2,128]{2,1,0:T(2,128)S(1)}, u32[]{:S(2)}, u32[]{:S(2)}) async-start(f32[32,2,128]{2,1,0:T(2,128)} %broadcast_in_dim.45), calls=%async_computation.6 | async-start | bytes 65536 | tf_op jit(solution)/shard_map/all_to_all | solution.py:18
  166.4 8.7 %all-to-all-done.6 = f32[32,2,128]{2,1,0:T(2,128)S(1)} async-done(((f32[32,2,128]{2,1,0:T(2,128)}), f32[32,2,128]{2,1,0:T(2,128)S(1)}, u32[]{:S(2)}, u32[]{:S(2)}) %all-to-all-start.6) | async-done | bytes 32800 | tf_op jit(solution)/shard_map/all_to_all | solution.py:18
  175.3 1.3 copy-done.13
  176.6 2.1 fusion.10
  179.4 12.0 %all_to_all.103 = f32[16,8,128]{2,1,0:T(8,128)S(1)} all-to-all(f32[16,8,128]{2,1,0:T(8,128)S(1)} %broadcast_in_dim.46), channel_id=1, replica_groups=mesh['gx'=32,'gy'=16] {'gy'}, dimensions={0} | all-to-all | bytes 131072 | tf_op jit(solution)/shard_map/all_to_all | solution.py:18
  192.3 3.9 %all-to-all-start.8 = ((f32[32,8,128]{2,1,0:T(8,128)}), f32[32,8,128]{2,1,0:T(8,128)S(1)}, u32[]{:S(2)}, u32[]{:S(2)}) async-start(f32[32,8,128]{2,1,0:T(8,128)} %fusion.57), calls=%async_computation.8 | async-start | bytes 262144 | tf_op jit(solution)/shard_map/all_to_all | solution.py:125
  197.2 8.1 %all-to-all-done.8 = f32[32,8,128]{2,1,0:T(8,128)S(1)} async-done(((f32[32,8,128]{2,1,0:T(8,128)}), f32[32,8,128]{2,1,0:T(8,128)S(1)}, u32[]{:S(2)}, u32[]{:S(2)}) %all-to-all-start.8) | async-done | bytes 131104 | tf_op jit(solution)/shard_map/all_to_all | solution.py:125
  206.9 3.9 %collective-permute-start.11 = (f32[2,128,128]{2,1,0:T(8,128)S(1)}, f32[2,128,128]{2,1,0:T(8,128)S(1)}, u32[]{:S(2)}, u32[]{:S(2)}) collective-permute-start(f32[2,128,128]{2,1,0:T(8,128)S(1)} %get-tuple-element.28), channel_id=1, source_target_pairs={{1,0},{2,1},{3,2},{4,3},{5,4},{6,5},{7,6},{8,7},{9,8},{10,9},{11,1... | collective-permute-start | bytes 393224 | tf_op jit(solution)/shard_map/ppermute | solution.py:12
  210.8 2.1 collective-permute-start.10
  212.9 1.3 collective-permute-start.9
  214.2 4.2 %collective-permute-start.8 = (f32[2,128,128]{2,1,0:T(8,128)S(1)}, f32[2,128,128]{2,1,0:T(8,128)S(1)}, u32[]{:S(2)}, u32[]{:S(2)}) collective-permute-start(f32[2,128,128]{2,1,0:T(8,128)S(1)} %get-tuple-element.26), channel_id=1, source_target_pairs={{0,16},{16,32},{32,48},{48,64},{64,80},{80,96},{96,112},{112,128},... | collective-permute-start | bytes 393224 | tf_op jit(solution)/shard_map/ppermute | solution.py:12
  218.4 10.7 %all_to_all.104 = f32[16,2,128]{2,1,0:T(2,128)S(1)} all-to-all(f32[16,2,128]{2,1,0:T(2,128)S(1)} %broadcast_in_dim.47), channel_id=1, replica_groups=mesh['gx'=32,'gy'=16] {'gy'}, dimensions={0} | all-to-all | bytes 32768 | tf_op jit(solution)/shard_map/all_to_all | solution.py:18
  231.1 5.2 %all-to-all-start.10 = ((f32[32,2,128]{2,1,0:T(2,128)}), f32[32,2,128]{2,1,0:T(2,128)S(1)}, u32[]{:S(2)}, u32[]{:S(2)}) async-start(f32[32,2,128]{2,1,0:T(2,128)} %broadcast_in_dim.48), calls=%async_computation.10 | async-start | bytes 65536 | tf_op jit(solution)/shard_map/all_to_all | solution.py:18
  236.3 8.7 %all-to-all-done.10 = f32[32,2,128]{2,1,0:T(2,128)S(1)} async-done(((f32[32,2,128]{2,1,0:T(2,128)}), f32[32,2,128]{2,1,0:T(2,128)S(1)}, u32[]{:S(2)}, u32[]{:S(2)}) %all-to-all-start.10) | async-done | bytes 32800 | tf_op jit(solution)/shard_map/all_to_all | solution.py:18
  246.5 2.1 fusion.11
  249.4 12.0 %all_to_all.105 = f32[16,8,128]{2,1,0:T(8,128)S(1)} all-to-all(f32[16,8,128]{2,1,0:T(8,128)S(1)} %broadcast_in_dim.49), channel_id=1, replica_groups=mesh['gx'=32,'gy'=16] {'gy'}, dimensions={0} | all-to-all | bytes 131072 | tf_op jit(solution)/shard_map/all_to_all | solution.py:18
  262.2 3.9 %all-to-all-start.12 = ((f32[32,8,128]{2,1,0:T(8,128)}), f32[32,8,128]{2,1,0:T(8,128)S(1)}, u32[]{:S(2)}, u32[]{:S(2)}) async-start(f32[32,8,128]{2,1,0:T(8,128)} %fusion.55), calls=%async_computation.12 | async-start | bytes 262144 | tf_op jit(solution)/shard_map/all_to_all | solution.py:125
  268.9 2.0 collective-permute-start.15
  270.9 3.5 %collective-permute-start.14 = (f32[2,128,128]{2,1,0:T(8,128)S(1)}, f32[2,128,128]{2,1,0:T(8,128)S(1)}, u32[]{:S(2)}, u32[]{:S(2)}) collective-permute-start(f32[2,128,128]{2,1,0:T(8,128)S(1)} %get-tuple-element.23), channel_id=1, source_target_pairs={{0,1},{1,2},{2,3},{3,4},{4,5},{5,6},{6,7},{7,8},{8,9},{9,10},{10,1... | collective-permute-start | bytes 393224 | tf_op jit(solution)/shard_map/ppermute | solution.py:12
  274.4 1.3 collective-permute-start.13
  275.7 4.0 %collective-permute-start.12 = (f32[2,128,128]{2,1,0:T(8,128)S(1)}, f32[2,128,128]{2,1,0:T(8,128)S(1)}, u32[]{:S(2)}, u32[]{:S(2)}) collective-permute-start(f32[2,128,128]{2,1,0:T(8,128)S(1)} %get-tuple-element.20), channel_id=1, source_target_pairs={{0,16},{16,32},{32,48},{48,64},{64,80},{80,96},{96,112},{112,128},... | collective-permute-start | bytes 393224 | tf_op jit(solution)/shard_map/ppermute | solution.py:12
  280.8 3.5 %all-to-all-start.13 = ((f32[16,2,128]{2,1,0:T(2,128)}), f32[16,2,128]{2,1,0:T(2,128)S(1)}, u32[]{:S(2)}, u32[]{:S(2)}) async-start(f32[16,2,128]{2,1,0:T(2,128)} %broadcast_in_dim.50), calls=%async_computation.13 | async-start | bytes 32768 | tf_op jit(solution)/shard_map/all_to_all | solution.py:18
  285.7 6.0 %all-to-all-done.13 = f32[16,2,128]{2,1,0:T(2,128)S(1)} async-done(((f32[16,2,128]{2,1,0:T(2,128)}), f32[16,2,128]{2,1,0:T(2,128)S(1)}, u32[]{:S(2)}, u32[]{:S(2)}) %all-to-all-start.13) | async-done | bytes 16416 | tf_op jit(solution)/shard_map/all_to_all | solution.py:18
  292.3 9.2 %all-to-all-start.14 = ((f32[32,2,128]{2,1,0:T(2,128)}), f32[32,2,128]{2,1,0:T(2,128)S(1)}, u32[]{:S(2)}, u32[]{:S(2)}) async-start(f32[32,2,128]{2,1,0:T(2,128)} %broadcast_in_dim.51), calls=%async_computation.14 | async-start | bytes 65536 | tf_op jit(solution)/shard_map/all_to_all | solution.py:18
  301.6 8.7 %all-to-all-done.14 = f32[32,2,128]{2,1,0:T(2,128)S(1)} async-done(((f32[32,2,128]{2,1,0:T(2,128)}), f32[32,2,128]{2,1,0:T(2,128)S(1)}, u32[]{:S(2)}, u32[]{:S(2)}) %all-to-all-start.14) | async-done | bytes 32800 | tf_op jit(solution)/shard_map/all_to_all | solution.py:18
  312.0 1.6 fusion.4
  (161 shorter events, 43.6 us)
Async XLA Ops:
  0.6 99.0 %copy-start = (bf16[1,1,4,128,128]{4,3,2,1,0:T(8,128)(2,1)S(1)}, bf16[1,1,4,128,128]{4,3,2,1,0:T(8,128)(2,1)}, u32[]{:S(2)}) copy-start(bf16[1,1,4,128,128]{4,3,2,1,0:T(8,128)(2,1)} %param.15) | copy-start | bytes 393220
  0.6 14.6 %copy-start.6 = (s32[4096]{0:T(1024)S(1)}, s32[4096]{0:T(1024)}, u32[]{:S(2)}) copy-start(s32[4096]{0:T(1024)} %param.19) | copy-start | bytes 49156
  0.7 14.7 %copy-start.5 = (f32[8,4096]{1,0:T(8,128)S(1)}, f32[8,4096]{1,0:T(8,128)}, u32[]{:S(2)}) copy-start(f32[8,4096]{1,0:T(8,128)} %param.18) | copy-start | bytes 393220
  3.4 47.9 %all-to-all-start.1 = ((f32[16,8,128]{2,1,0:T(8,128)}), f32[16,8,128]{2,1,0:T(8,128)S(1)}, u32[]{:S(2)}, u32[]{:S(2)}) async-start(f32[16,8,128]{2,1,0:T(8,128)} %broadcast_in_dim.42), calls=%async_computation.1 | async-start | bytes 131072 | tf_op jit(solution)/shard_map/all_to_all | solution.py:18
  15.9 45.1 %copy-start.7 = (f32[1,1,896]{2,1,0:T(1,128)S(1)}, f32[1,1,896]{2,1,0:T(1,128)}, u32[]{:S(2)}) copy-start(f32[1,1,896]{2,1,0:T(1,128)} %param.14) | copy-start | bytes 10756
  30.1 45.5 %copy-start.9 = (s32[1,1,4,128]{3,2,1,0:T(4,128)S(1)}, s32[1,1,4,128]{3,2,1,0:T(4,128)}, u32[]{:S(2)}) copy-start(s32[1,1,4,128]{3,2,1,0:T(4,128)} %param.16) | copy-start | bytes 6148
  30.1 54.7 %copy-start.3 = (bf16[1,1,8,896]{3,2,1,0:T(8,128)(2,1)S(1)}, bf16[1,1,8,896]{3,2,1,0:T(8,128)(2,1)}, u32[]{:S(2)}) copy-start(bf16[1,1,8,896]{3,2,1,0:T(8,128)(2,1)} %param.17) | copy-start | bytes 43012
  30.1 54.7 %copy-start.4 = (bf16[1,1,896,128]{3,2,1,0:T(8,128)(2,1)S(1)}, bf16[1,1,896,128]{3,2,1,0:T(8,128)(2,1)}, u32[]{:S(2)}) copy-start(bf16[1,1,896,128]{3,2,1,0:T(8,128)(2,1)} %param.10) | copy-start | bytes 688132
  51.3 18.9 %all-to-all-start = ((f32[32,8,1,128]{3,1,2,0:T(8,128)}), f32[32,8,1,128]{3,1,2,0:T(8,128)S(1)}, u32[]{:S(2)}, u32[]{:S(2)}) async-start(f32[32,8,1,128]{3,1,2,0:T(8,128)} %constant_dynamic-update-slice_fusion), calls=%async_computation | async-start | bytes 262144 | tf_op jit(solution)/shard_map/all_to_all | solution.py:75
  71.0 13.7 %all-to-all-start.2 = ((f32[32,8,128]{2,1,0:T(8,128)}), f32[32,8,128]{2,1,0:T(8,128)S(1)}, u32[]{:S(2)}, u32[]{:S(2)}) async-start(f32[32,8,128]{2,1,0:T(8,128)} %fusion.61), calls=%async_computation.2 | async-start | bytes 262144 | tf_op jit(solution)/shard_map/all_to_all | solution.py:125
  84.7 15.5 %copy-start.8 = (f32[1,1,896]{2,1,0:T(1,128)S(1)}, f32[1,1,896]{2,1,0:T(1,128)}, u32[]{:S(2)}) copy-start(f32[1,1,896]{2,1,0:T(1,128)} %param.12) | copy-start | bytes 10756
  86.5 14.3 %collective-permute-start.3 = (bf16[128,128]{1,0:T(8,128)(2,1)S(1)}, bf16[128,128]{1,0:T(8,128)(2,1)S(1)}, u32[]{:S(2)}, u32[]{:S(2)}) collective-permute-start(bf16[128,128]{1,0:T(8,128)(2,1)S(1)} %get-tuple-element.40), channel_id=1, source_target_pairs={{1,0},{2,1},{3,2},{4,3},{5,4},{6,5},{7,6},{8,7},{9,8},{10,9},{11,1... | collective-permute-start | bytes 98312 | tf_op jit(solution)/shard_map/ppermute | solution.py:12
  91.1 9.7 %collective-permute-start.2 = (bf16[128,128]{1,0:T(8,128)(2,1)S(1)}, bf16[128,128]{1,0:T(8,128)(2,1)S(1)}, u32[]{:S(2)}, u32[]{:S(2)}) collective-permute-start(bf16[128,128]{1,0:T(8,128)(2,1)S(1)} %get-tuple-element.38), channel_id=1, source_target_pairs={{0,1},{1,2},{2,3},{3,4},{4,5},{5,6},{6,7},{7,8},{8,9},{9,10},{10,1... | collective-permute-start | bytes 98312 | tf_op jit(solution)/shard_map/ppermute | solution.py:12
  94.3 6.5 %collective-permute-start.1 = (bf16[128,128]{1,0:T(8,128)(2,1)S(1)}, bf16[128,128]{1,0:T(8,128)(2,1)S(1)}, u32[]{:S(2)}, u32[]{:S(2)}) collective-permute-start(bf16[128,128]{1,0:T(8,128)(2,1)S(1)} %get-tuple-element.39), channel_id=1, source_target_pairs={{16,0},{32,16},{48,32},{64,48},{80,64},{96,80},{112,96},{128,112},... | collective-permute-start | bytes 98312 | tf_op jit(solution)/shard_map/ppermute | solution.py:12
  95.6 5.2 %collective-permute-start = (bf16[128,128]{1,0:T(8,128)(2,1)S(1)}, bf16[128,128]{1,0:T(8,128)(2,1)S(1)}, u32[]{:S(2)}, u32[]{:S(2)}) collective-permute-start(bf16[128,128]{1,0:T(8,128)(2,1)S(1)} %get-tuple-element.37), channel_id=1, source_target_pairs={{0,16},{16,32},{32,48},{48,64},{64,80},{80,96},{96,112},{112,128},... | collective-permute-start | bytes 98312 | tf_op jit(solution)/shard_map/ppermute | solution.py:12
  100.8 2.6 copy-start.1
  100.9 2.6 copy-start.10
  119.4 16.5 %all-to-all-start.4 = ((f32[32,8,128]{2,1,0:T(8,128)}), f32[32,8,128]{2,1,0:T(8,128)S(1)}, u32[]{:S(2)}, u32[]{:S(2)}) async-start(f32[32,8,128]{2,1,0:T(8,128)} %fusion.59), calls=%async_computation.4 | async-start | bytes 262144 | tf_op jit(solution)/shard_map/all_to_all | solution.py:125
  137.4 22.2 %collective-permute-start.7 = (f32[2,128,128]{2,1,0:T(8,128)S(1)}, f32[2,128,128]{2,1,0:T(8,128)S(1)}, u32[]{:S(2)}, u32[]{:S(2)}) collective-permute-start(f32[2,128,128]{2,1,0:T(8,128)S(1)} %get-tuple-element.34), channel_id=1, source_target_pairs={{1,0},{2,1},{3,2},{4,3},{5,4},{6,5},{7,6},{8,7},{9,8},{10,9},{11,1... | collective-permute-start | bytes 393224 | tf_op jit(solution)/shard_map/ppermute | solution.py:12
  141.5 18.2 %collective-permute-start.6 = (f32[2,128,128]{2,1,0:T(8,128)S(1)}, f32[2,128,128]{2,1,0:T(8,128)S(1)}, u32[]{:S(2)}, u32[]{:S(2)}) collective-permute-start(f32[2,128,128]{2,1,0:T(8,128)S(1)} %get-tuple-element.35), channel_id=1, source_target_pairs={{0,1},{1,2},{2,3},{3,4},{4,5},{5,6},{6,7},{7,8},{8,9},{9,10},{10,1... | collective-permute-start | bytes 393224 | tf_op jit(solution)/shard_map/ppermute | solution.py:12
  143.5 16.1 %collective-permute-start.5 = (f32[2,128,128]{2,1,0:T(8,128)S(1)}, f32[2,128,128]{2,1,0:T(8,128)S(1)}, u32[]{:S(2)}, u32[]{:S(2)}) collective-permute-start(f32[2,128,128]{2,1,0:T(8,128)S(1)} %get-tuple-element.33), channel_id=1, source_target_pairs={{16,0},{32,16},{48,32},{64,48},{80,64},{96,80},{112,96},{128,112},... | collective-permute-start | bytes 393224 | tf_op jit(solution)/shard_map/ppermute | solution.py:12
  144.8 14.8 %collective-permute-start.4 = (f32[2,128,128]{2,1,0:T(8,128)S(1)}, f32[2,128,128]{2,1,0:T(8,128)S(1)}, u32[]{:S(2)}, u32[]{:S(2)}) collective-permute-start(f32[2,128,128]{2,1,0:T(8,128)S(1)} %get-tuple-element.32), channel_id=1, source_target_pairs={{0,16},{16,32},{32,48},{48,64},{64,80},{80,96},{96,112},{112,128},... | collective-permute-start | bytes 393224 | tf_op jit(solution)/shard_map/ppermute | solution.py:12
  161.6 13.6 %all-to-all-start.6 = ((f32[32,2,128]{2,1,0:T(2,128)}), f32[32,2,128]{2,1,0:T(2,128)S(1)}, u32[]{:S(2)}, u32[]{:S(2)}) async-start(f32[32,2,128]{2,1,0:T(2,128)} %broadcast_in_dim.45), calls=%async_computation.6 | async-start | bytes 65536 | tf_op jit(solution)/shard_map/all_to_all | solution.py:18
  175.2 1.4 copy-start.13
  176.6 2.1 copy-start.11
  192.3 13.0 %all-to-all-start.8 = ((f32[32,8,128]{2,1,0:T(8,128)}), f32[32,8,128]{2,1,0:T(8,128)S(1)}, u32[]{:S(2)}, u32[]{:S(2)}) async-start(f32[32,8,128]{2,1,0:T(8,128)} %fusion.57), calls=%async_computation.8 | async-start | bytes 262144 | tf_op jit(solution)/shard_map/all_to_all | solution.py:125
  206.9 22.3 %collective-permute-start.11 = (f32[2,128,128]{2,1,0:T(8,128)S(1)}, f32[2,128,128]{2,1,0:T(8,128)S(1)}, u32[]{:S(2)}, u32[]{:S(2)}) collective-permute-start(f32[2,128,128]{2,1,0:T(8,128)S(1)} %get-tuple-element.28), channel_id=1, source_target_pairs={{1,0},{2,1},{3,2},{4,3},{5,4},{6,5},{7,6},{8,7},{9,8},{10,9},{11,1... | collective-permute-start | bytes 393224 | tf_op jit(solution)/shard_map/ppermute | solution.py:12
  210.8 18.3 %collective-permute-start.10 = (f32[2,128,128]{2,1,0:T(8,128)S(1)}, f32[2,128,128]{2,1,0:T(8,128)S(1)}, u32[]{:S(2)}, u32[]{:S(2)}) collective-permute-start(f32[2,128,128]{2,1,0:T(8,128)S(1)} %get-tuple-element.29), channel_id=1, source_target_pairs={{0,1},{1,2},{2,3},{3,4},{4,5},{5,6},{6,7},{7,8},{8,9},{9,10},{10,1... | collective-permute-start | bytes 393224 | tf_op jit(solution)/shard_map/ppermute | solution.py:12
  212.9 16.3 %collective-permute-start.9 = (f32[2,128,128]{2,1,0:T(8,128)S(1)}, f32[2,128,128]{2,1,0:T(8,128)S(1)}, u32[]{:S(2)}, u32[]{:S(2)}) collective-permute-start(f32[2,128,128]{2,1,0:T(8,128)S(1)} %get-tuple-element.27), channel_id=1, source_target_pairs={{16,0},{32,16},{48,32},{64,48},{80,64},{96,80},{112,96},{128,112},... | collective-permute-start | bytes 393224 | tf_op jit(solution)/shard_map/ppermute | solution.py:12
  214.2 15.0 %collective-permute-start.8 = (f32[2,128,128]{2,1,0:T(8,128)S(1)}, f32[2,128,128]{2,1,0:T(8,128)S(1)}, u32[]{:S(2)}, u32[]{:S(2)}) collective-permute-start(f32[2,128,128]{2,1,0:T(8,128)S(1)} %get-tuple-element.26), channel_id=1, source_target_pairs={{0,16},{16,32},{32,48},{48,64},{64,80},{80,96},{96,112},{112,128},... | collective-permute-start | bytes 393224 | tf_op jit(solution)/shard_map/ppermute | solution.py:12
  231.1 13.9 %all-to-all-start.10 = ((f32[32,2,128]{2,1,0:T(2,128)}), f32[32,2,128]{2,1,0:T(2,128)S(1)}, u32[]{:S(2)}, u32[]{:S(2)}) async-start(f32[32,2,128]{2,1,0:T(2,128)} %broadcast_in_dim.48), calls=%async_computation.10 | async-start | bytes 65536 | tf_op jit(solution)/shard_map/all_to_all | solution.py:18
  245.1 1.4 copy-start.14
  246.5 2.1 copy-start.12
  262.2 17.5 %all-to-all-start.12 = ((f32[32,8,128]{2,1,0:T(8,128)}), f32[32,8,128]{2,1,0:T(8,128)S(1)}, u32[]{:S(2)}, u32[]{:S(2)}) async-start(f32[32,8,128]{2,1,0:T(8,128)} %fusion.55), calls=%async_computation.12 | async-start | bytes 262144 | tf_op jit(solution)/shard_map/all_to_all | solution.py:125
  268.9 15.5 %collective-permute-start.15 = (f32[2,128,128]{2,1,0:T(8,128)}, f32[2,128,128]{2,1,0:T(8,128)S(1)}, u32[]{:S(2)}, u32[]{:S(2)}) collective-permute-start(f32[2,128,128]{2,1,0:T(8,128)} %get-tuple-element.22), channel_id=1, source_target_pairs={{1,0},{2,1},{3,2},{4,3},{5,4},{6,5},{7,6},{8,7},{9,8},{10,9},{11,1... | collective-permute-start | bytes 393224 | tf_op jit(solution)/shard_map/ppermute | solution.py:12
  270.9 13.4 %collective-permute-start.14 = (f32[2,128,128]{2,1,0:T(8,128)S(1)}, f32[2,128,128]{2,1,0:T(8,128)S(1)}, u32[]{:S(2)}, u32[]{:S(2)}) collective-permute-start(f32[2,128,128]{2,1,0:T(8,128)S(1)} %get-tuple-element.23), channel_id=1, source_target_pairs={{0,1},{1,2},{2,3},{3,4},{4,5},{5,6},{6,7},{7,8},{8,9},{9,10},{10,1... | collective-permute-start | bytes 393224 | tf_op jit(solution)/shard_map/ppermute | solution.py:12
  274.4 9.9 %collective-permute-start.13 = (f32[2,128,128]{2,1,0:T(8,128)S(1)}, f32[2,128,128]{2,1,0:T(8,128)S(1)}, u32[]{:S(2)}, u32[]{:S(2)}) collective-permute-start(f32[2,128,128]{2,1,0:T(8,128)S(1)} %get-tuple-element.21), channel_id=1, source_target_pairs={{16,0},{32,16},{48,32},{64,48},{80,64},{96,80},{112,96},{128,112},... | collective-permute-start | bytes 393224 | tf_op jit(solution)/shard_map/ppermute | solution.py:12
  275.7 8.6 %collective-permute-start.12 = (f32[2,128,128]{2,1,0:T(8,128)S(1)}, f32[2,128,128]{2,1,0:T(8,128)S(1)}, u32[]{:S(2)}, u32[]{:S(2)}) collective-permute-start(f32[2,128,128]{2,1,0:T(8,128)S(1)} %get-tuple-element.20), channel_id=1, source_target_pairs={{0,16},{16,32},{32,48},{48,64},{64,80},{80,96},{96,112},{112,128},... | collective-permute-start | bytes 393224 | tf_op jit(solution)/shard_map/ppermute | solution.py:12
  280.8 10.9 %all-to-all-start.13 = ((f32[16,2,128]{2,1,0:T(2,128)}), f32[16,2,128]{2,1,0:T(2,128)S(1)}, u32[]{:S(2)}, u32[]{:S(2)}) async-start(f32[16,2,128]{2,1,0:T(2,128)} %broadcast_in_dim.50), calls=%async_computation.13 | async-start | bytes 32768 | tf_op jit(solution)/shard_map/all_to_all | solution.py:18
  284.4 26.8 %copy-start.2 = (bf16[896,512]{1,0:T(8,128)(2,1)S(1)}, bf16[896,512]{1,0:T(8,128)(2,1)}, u32[]{:S(2)}) copy-start(bf16[896,512]{1,0:T(8,128)(2,1)} %copy-done.1) | copy-start | bytes 2752516
  292.3 18.0 %all-to-all-start.14 = ((f32[32,2,128]{2,1,0:T(2,128)}), f32[32,2,128]{2,1,0:T(2,128)S(1)}, u32[]{:S(2)}, u32[]{:S(2)}) async-start(f32[32,2,128]{2,1,0:T(2,128)} %broadcast_in_dim.51), calls=%async_computation.14 | async-start | bytes 65536 | tf_op jit(solution)/shard_map/all_to_all | solution.py:18
  310.4 1.6 copy-start.15
